TPU v7x, 32 devices: a whole 2x2x4 slice. The times are simulated.
32 devices in a mesh: region: 4 (over z), sub: 8 (over y, x, core).
Axes of the slice: x: 2, y: 2, z: 4, core: 2. Of those that a mesh axis runs over, the one named last changes fastest.
Arguments:
- feats: bfloat16 [16384, 1536], P(('region', 'sub')), may hold values from -6 to 6
- conv_weight: bfloat16 [192, 128], replicated, may hold values from -0.4375 to 0.4375
- conv_bias: float32 [128], replicated, may hold values from -3 to 3
- theta: bfloat16 [64, 64], replicated, may hold values from -0.75 to 0.75
- edge_weight: float32 [4096], P(('region', 'sub')), may hold values from 1 to 4
- inner_edge: int32 [16384, 2], P(('region', 'sub')), may hold values from 0 to 127
- crossing_segment: int32 [4096], P(('region', 'sub')), may hold values from 0 to 511
- cut_dest: int32 [4096, 1], P(('region', 'sub')), may hold values from 0 to 31; in each aligned block of 128 rows (0 to 127, 128 to 255, ...) at most 8 rows name the same one
- crossing_hyperedge: int32 [4096], P(('region', 'sub')), may hold values from 0 to 127
- cotangent: bfloat16 [16384, 1280], P(('region', 'sub')), may hold values from -6 to 6
Outputs:
- block_out: bfloat16 [16384, 1280], P(('region', 'sub'))
- grad_feats: bfloat16 [16384, 1536], P(('region', 'sub'))
- grad_conv: float32 [192, 128], replicated
- grad_bias: float32 [128], replicated
- grad_theta: float32 [64, 64], replicated
Inputs may be any that keep to these rules, and one draw needn't show every extreme that they name: `cut_dest`: among the 128 cut memberships of one device no owner is named more than 8 times; in some device one owner is named exactly 8 times.
All inputs are finite; a program needn't handle non-finite values.
Results may differ from a plain program's by a relative error of at most 0.0072.
Values may be sent and summed in bfloat16 or wider, within the bound.
No kernel may reach another device: no remote copies, remote signals or barrier semaphores. Data moves between devices by JAX's collectives and lax.ppermute only.
A program may use at most 64 MiB of HBM per device.

v0:
```python
import jax
import jax.numpy as jnp
from jax import lax
from jax.sharding import PartitionSpec as P

C = 64
T_SIZE = 12
B = 2
KT = 3
MEM = 2
TP = 10
EDGE_DEV = 128


def body(
    feats,
    conv_weight,
    conv_bias,
    theta,
    edge_weight,
    inner_edge,
    crossing_segment,
    cut_dest,
    crossing_hyperedge,
    cotangent,
):
    seg = feats.shape[0]
    n_region = lax.axis_size("region")
    n_sub = lax.axis_size("sub")
    device_list = n_region * n_sub
    slot_capacity = max(2, 2 * crossing_segment.shape[0] // device_list)
    slot_total = device_list * slot_capacity
    width = TP * B * C
    x4 = feats.reshape(seg, T_SIZE, B, C)
    stack = jnp.concatenate([x4[:, k : k + TP] for k in range(KT)], axis=-1)
    u = (
        jnp.einsum("stbk,kf->stbf", stack, conv_weight, preferred_element_type=jnp.float32)
        + conv_bias
    )
    gate = jax.nn.sigmoid(u[..., C:])
    first = u[..., :C]
    hidden = (first * gate).astype(jnp.bfloat16)
    z = (
        jnp.einsum("stbc,cd->stbd", hidden, theta, preferred_element_type=jnp.float32)
        .astype(jnp.bfloat16)
        .reshape(seg, width)
    )
    edge_index = jnp.arange(EDGE_DEV, dtype=jnp.int32)
    incidence = jnp.zeros((EDGE_DEV, seg), jnp.float32)
    for m in range(MEM):
        incidence = incidence + (inner_edge[:, m][None, :] == edge_index[:, None]).astype(
            jnp.float32
        )
    inner_count = jnp.sum(incidence, axis=1)
    incidence = incidence.astype(jnp.bfloat16)
    dest = cut_dest[:, 0]
    dest_hot = (dest[:, None] == jnp.arange(device_list, dtype=jnp.int32)[None, :]).astype(
        jnp.int32
    )
    rank = jnp.sum((jnp.cumsum(dest_hot, axis=0) - 1) * dest_hot, axis=1)
    slot_position = dest * slot_capacity + rank
    slotted_segment = jnp.full((slot_total,), -1, jnp.int32).at[slot_position].set(crossing_segment)
    slotted_hyperedge = (
        jnp.full((slot_total,), -1, jnp.int32).at[slot_position].set(crossing_hyperedge)
    )
    members = (slotted_segment[None, :] == jnp.arange(seg, dtype=jnp.int32)[:, None]).astype(
        jnp.float32
    )
    degree = (MEM + jnp.sum(members, axis=1))[:, None]
    members = members.astype(jnp.bfloat16)

    def pick_slots(rows):
        return jnp.einsum("sn,sf->nf", members, rows, preferred_element_type=jnp.float32).astype(
            jnp.bfloat16
        )

    send = pick_slots(z)
    recv, recv_edge = (
        lax.all_to_all(send, ("region", "sub"), split_axis=0, concat_axis=0, tiled=True),
        lax.all_to_all(
            slotted_hyperedge, ("region", "sub"), split_axis=0, concat_axis=0, tiled=True
        ),
    )
    owned = (recv_edge[None, :] == edge_index[:, None]).astype(jnp.float32)
    count = 1.0 + inner_count + jnp.sum(owned, axis=1)
    owned = owned.astype(jnp.bfloat16)
    scale = (edge_weight / count)[:, None]

    def edge_side(local_rows, arrived):
        total = jnp.dot(incidence, local_rows, preferred_element_type=jnp.float32) + jnp.dot(
            owned, arrived, preferred_element_type=jnp.float32
        )
        values = (scale * total).astype(jnp.bfloat16)
        returned = jnp.einsum(
            "en,ef->nf", owned, values, preferred_element_type=jnp.float32
        ).astype(jnp.bfloat16)
        return (values, returned)

    def member_side(values, back):
        return jnp.einsum(
            "es,ef->sf", incidence, values, preferred_element_type=jnp.float32
        ) + jnp.dot(members, back, preferred_element_type=jnp.float32)

    edge_val, ret_rows = edge_side(z, recv)
    back = lax.all_to_all(ret_rows, ("region", "sub"), split_axis=0, concat_axis=0, tiled=True)
    y = member_side(edge_val, back) / degree
    sig_y = jax.nn.sigmoid(y)
    block_out = (y * sig_y).astype(jnp.bfloat16)
    dy = cotangent.astype(jnp.float32) * sig_y * (1.0 + y * (1.0 - sig_y))
    grad_rows = (dy / degree).astype(jnp.bfloat16)
    send_grads = pick_slots(grad_rows)
    recv_grads = lax.all_to_all(
        send_grads, ("region", "sub"), split_axis=0, concat_axis=0, tiled=True
    )
    dedge, ret_grads = edge_side(grad_rows, recv_grads)
    back_grads = lax.all_to_all(
        ret_grads, ("region", "sub"), split_axis=0, concat_axis=0, tiled=True
    )
    dz = member_side(dedge, back_grads).astype(jnp.bfloat16).reshape(seg, TP, B, C)
    g_theta = jnp.einsum("stbc,stbd->cd", hidden, dz, preferred_element_type=jnp.float32)
    dh = jnp.einsum("stbd,cd->stbc", dz, theta, preferred_element_type=jnp.float32)
    du = jnp.concatenate([dh * gate, dh * first * gate * (1.0 - gate)], axis=-1).astype(
        jnp.bfloat16
    )
    g_conv = jnp.einsum("stbk,stbf->kf", stack, du, preferred_element_type=jnp.float32)
    g_bias = jnp.sum(du.astype(jnp.float32), axis=(0, 1, 2))
    sum_conv, sum_bias, sum_theta = lax.psum((g_conv, g_bias, g_theta), ("region", "sub"))
    norm = 1.0 / jnp.sqrt(jnp.float32(seg * device_list * TP * B))
    dstack = jnp.einsum("stbf,kf->stbk", du, conv_weight, preferred_element_type=jnp.float32)
    grad_sum = jnp.zeros((seg, T_SIZE, B, C), jnp.float32)
    for k in range(KT):
        grad_sum = grad_sum + jnp.pad(
            dstack[..., k * C : (k + 1) * C], ((0, 0), (k, KT - 1 - k), (0, 0), (0, 0))
        )
    grad_feats = grad_sum.astype(jnp.bfloat16).reshape(seg, T_SIZE * B * C)
    return (block_out, grad_feats, sum_conv * norm, sum_bias * norm, sum_theta * norm)


def solution(mesh):
    in_specs = (
        P(("region", "sub"), None),
        P(),
        P(),
        P(),
        P(("region", "sub")),
        P(("region", "sub"), None),
        P(("region", "sub")),
        P(("region", "sub"), None),
        P(("region", "sub")),
        P(("region", "sub"), None),
    )
    out_specs = (P(("region", "sub"), None), P(("region", "sub"), None), P(), P(), P())
    return jax.shard_map(body, mesh=mesh, in_specs=in_specs, out_specs=out_specs, check_vma=False)
```

profile of v0, /device:TPU:8, one launch (start us, length us, event | category | flops | bytes accessed | tf_op | source)
XLA Modules:
  0.0 271.4 jit_solution(6056330176690974189)
XLA Ops:
  11.4 6.0 %all-to-all-start = ((s32[32,8,1]{1,2,0:T(1,128)}), s32[32,8,1]{1,2,0:T(1,128)S(1)}, u32[]{:S(2)}, u32[]{:S(2)}) async-start(s32[32,8,1]{1,2,0:T(1,128)} %bitcast.5), calls=%async_computation | async-start | bytes 32768 | tf_op jit(solution)/shard_map/all_to_all | solution.py:80
  18.6 1.7 copy.44
  23.5 1.6 copy-done.1
  26.2 1.4 fusion.10
  27.6 5.8 %all-to-all-start.1 = ((bf16[32,8,1280]{2,1,0:T(8,128)(2,1)}), bf16[32,8,1280]{2,1,0:T(8,128)(2,1)S(1)}, u32[]{:S(2)}, u32[]{:S(2)}) async-start(bf16[32,8,1280]{2,1,0:T(8,128)(2,1)} %fusion.10), calls=%async_computation.1 | async-start | bytes 1310720 | tf_op jit(solution)/shard_map/all_to_all | solution.py:79
  35.6 15.4 %all-to-all-done.1 = bf16[32,8,1280]{2,1,0:T(8,128)(2,1)S(1)} async-done(((bf16[32,8,1280]{2,1,0:T(8,128)(2,1)}), bf16[32,8,1280]{2,1,0:T(8,128)(2,1)S(1)}, u32[]{:S(2)}, u32[]{:S(2)}) %all-to-all-start.1) | async-done | bytes 655392 | tf_op jit(solution)/shard_map/all_to_all | solution.py:79
  52.4 3.8 %all-to-all-start.2 = ((bf16[32,8,1280]{2,1,0:T(8,128)(2,1)}), bf16[32,8,1280]{2,1,0:T(8,128)(2,1)S(1)}, u32[]{:S(2)}, u32[]{:S(2)}) async-start(bf16[32,8,1280]{2,1,0:T(8,128)(2,1)} %fusion.11), calls=%async_computation.2 | async-start | bytes 1310720 | tf_op jit(solution)/shard_map/all_to_all | solution.py:105
  56.5 2.0 fusion.43
  58.5 15.4 %all-to-all-done.2 = bf16[32,8,1280]{2,1,0:T(8,128)(2,1)S(1)} async-done(((bf16[32,8,1280]{2,1,0:T(8,128)(2,1)}), bf16[32,8,1280]{2,1,0:T(8,128)(2,1)S(1)}, u32[]{:S(2)}, u32[]{:S(2)}) %all-to-all-start.2) | async-done | bytes 655392 | tf_op jit(solution)/shard_map/all_to_all | solution.py:105
  73.9 4.1 %divide_convert_fusion = (bf16[512,1280]{1,0:T(8,128)(2,1)S(1)}, bf16[512,1280]{1,0:T(8,128)(2,1)}) fusion(bf16[512,1280]{1,0:T(8,128)(2,1)} %param.19, f32[512]{0:T(512)S(1)} %broadcast_add_fusion.1, f32[512,1280]{1,0:T(8,128)} %fusion.43, bf16[32,8,1280]{2,1,0:T(8,128)(2,1)S(1)} %all-to-all-done.2, s32[256]{0:T(256)S(1)} %scatter_custom_fusion.1), kind=kOutput, calls=%fused_computation.19 | convolution fusion | flops 345767936 | bytes 7212032 | tf_op jit(solution)/shard_map/dot_general | solution.py:102
  79.3 3.8 %all-to-all-start.3 = ((bf16[32,8,1280]{2,1,0:T(8,128)(2,1)}), bf16[32,8,1280]{2,1,0:T(8,128)(2,1)S(1)}, u32[]{:S(2)}, u32[]{:S(2)}) async-start(bf16[32,8,1280]{2,1,0:T(8,128)(2,1)} %fusion.12), calls=%async_computation.3 | async-start | bytes 1310720 | tf_op jit(solution)/shard_map/all_to_all | solution.py:112
  83.5 17.2 %all-to-all-done.3 = bf16[32,8,1280]{2,1,0:T(8,128)(2,1)S(1)} async-done(((bf16[32,8,1280]{2,1,0:T(8,128)(2,1)}), bf16[32,8,1280]{2,1,0:T(8,128)(2,1)S(1)}, u32[]{:S(2)}, u32[]{:S(2)}) %all-to-all-start.3) | async-done | bytes 655392 | tf_op jit(solution)/shard_map/all_to_all | solution.py:112
  102.2 3.9 %all-to-all-start.4 = ((bf16[32,8,1280]{2,1,0:T(8,128)(2,1)}), bf16[32,8,1280]{2,1,0:T(8,128)(2,1)}, u32[]{:S(2)}, u32[]{:S(2)}) async-start(bf16[32,8,1280]{2,1,0:T(8,128)(2,1)} %fusion.13), calls=%async_computation.4 | async-start | bytes 1310720 | tf_op jit(solution)/shard_map/all_to_all | solution.py:116
  106.9 16.9 %all-to-all-done.4 = bf16[32,8,1280]{2,1,0:T(8,128)(2,1)} async-done(((bf16[32,8,1280]{2,1,0:T(8,128)(2,1)}), bf16[32,8,1280]{2,1,0:T(8,128)(2,1)}, u32[]{:S(2)}, u32[]{:S(2)}) %all-to-all-start.4) | async-done | bytes 655392 | tf_op jit(solution)/shard_map/all_to_all | solution.py:116
  123.8 2.7 fusion.3
  126.4 2.4 copy.46
  128.9 4.3 %multiply_convert_fusion.1 = (bf16[512,10,2,64]{0,3,2,1:T(8,128)(2,1)S(1)}, bf16[512,10,2,64]{0,3,2,1:T(8,128)(2,1)S(1)}) fusion(f32[512,10,2,128]{0,3,2,1:T(8,128)} %copy-done.1, bf16[512,10,2,64]{0,3,2,1:T(8,128)(2,1)} %bitcast.78, bf16[64,64]{1,0:T(8,128)(2,1)S(1)} %copy-done.11), kind=kOutput, calls=%fused_computation.18 | convolution fusion | flops 90439680 | bytes 9183232 | tf_op jit(solution)/shard_map/stbd,cd->stbc/dot_general | solution.py:121
  134.9 1.8 fusion.19
  137.2 4.2 %fusion.60 = f32[512,10,2,192]{0,3,2,1:T(8,128)} fusion(bf16[192,128]{1,0:T(8,128)(2,1)S(1)} %copy-done, bf16[512,10,2,64]{0,3,2,1:T(8,128)(2,1)S(1)} %get-tuple-element.31, bf16[512,10,2,64]{0,3,2,1:T(8,128)(2,1)S(1)} %get-tuple-element.30), kind=kOutput, calls=%fused_computation.82 | convolution fusion | flops 508559360 | bytes 10534912 | tf_op jit(solution)/shard_map/stbf,kf->stbk/dot_general | solution.py:129
  141.5 39.5 %all-reduce.3 = (f32[128]{0:T(128)S(1)}, f32[64,64]{1,0:T(8,128)S(1)}) all-reduce(f32[128]{0:T(128)S(1)} %convert_reduce_fusion, f32[64,64]{1,0:T(8,128)S(1)} %fusion.24), channel_id=1, replica_groups=mesh['region'=4,'sub'=8] {'region','sub'}, use_global_device_ids=true, to_apply=%region_9.10 | all-reduce | flops 4224 | bytes 33792 | tf_op jit(solution)/shard_map/psum | solution.py:127
  182.2 4.4 %fusion.71 = (f32[512,10,2,64]{0,3,2,1:T(8,128)S(1)}, f32[512,10,2,64]{0,3,2,1:T(8,128)S(1)}, f32[512,10,2,64]{0,3,2,1:T(8,128)S(1)}) fusion(f32[512,10,2,192]{0,3,2,1:T(8,128)} %fusion.60), kind=kLoop, calls=%fused_computation.100 | loop fusion | bytes 15728640 | tf_op jit(solution)/shard_map/slice | solution.py:133
  187.6 1.6 copy.52
  189.2 73.8 %all-reduce.6.cloned.1.call-done = f32[192,128]{1,0:T(8,128)} async-done(((f32[192,128]{1,0:T(8,128)}), f32[192,128]{1,0:T(8,128)}) %all-reduce.6.cloned.1.call-update) | async-done | bytes 98320 | tf_op jit(solution)/shard_map/psum | solution.py:127
  263.0 1.5 broadcast_multiply_fusion
  (65 shorter events, 21.5 us)
Async XLA Ops:
  7.2 13.7 %copy-start = (bf16[192,128]{1,0:T(8,128)(2,1)S(1)}, bf16[192,128]{1,0:T(8,128)(2,1)}, u32[]{:S(2)}) copy-start(bf16[192,128]{1,0:T(8,128)(2,1)} %param.11) | copy-start | bytes 147460
  11.4 16.1 %all-to-all-start = ((s32[32,8,1]{1,2,0:T(1,128)}), s32[32,8,1]{1,2,0:T(1,128)S(1)}, u32[]{:S(2)}, u32[]{:S(2)}) async-start(s32[32,8,1]{1,2,0:T(1,128)} %bitcast.5), calls=%async_computation | async-start | bytes 32768 | tf_op jit(solution)/shard_map/all_to_all | solution.py:80
  20.3 0.7 copy-start.14
  20.8 1.2 copy-start.5
  20.8 1.5 copy-start.7
  20.8 1.9 copy-start.9
  22.7 2.3 copy-start.1
  22.7 2.3 copy-start.11
  25.0 1.1 copy-start.2
  25.0 8.4 %copy-start.12 = (s32[512,2]{0,1:T(2,128)S(1)}, s32[512,2]{0,1:T(2,128)}, u32[]{:S(2)}) copy-start(s32[512,2]{0,1:T(2,128)} %param.15) | copy-start | bytes 12292
  26.2 9.4 %copy-start.13 = (f32[128]{0:T(128)S(1)}, f32[128]{0:T(128)}, u32[]{:S(2)}) copy-start(f32[128]{0:T(128)} %param.14) | copy-start | bytes 1540
  27.6 23.4 %all-to-all-start.1 = ((bf16[32,8,1280]{2,1,0:T(8,128)(2,1)}), bf16[32,8,1280]{2,1,0:T(8,128)(2,1)S(1)}, u32[]{:S(2)}, u32[]{:S(2)}) async-start(bf16[32,8,1280]{2,1,0:T(8,128)(2,1)} %fusion.10), calls=%async_computation.1 | async-start | bytes 1310720 | tf_op jit(solution)/shard_map/all_to_all | solution.py:79
  52.4 21.4 %all-to-all-start.2 = ((bf16[32,8,1280]{2,1,0:T(8,128)(2,1)}), bf16[32,8,1280]{2,1,0:T(8,128)(2,1)S(1)}, u32[]{:S(2)}, u32[]{:S(2)}) async-start(bf16[32,8,1280]{2,1,0:T(8,128)(2,1)} %fusion.11), calls=%async_computation.2 | async-start | bytes 1310720 | tf_op jit(solution)/shard_map/all_to_all | solution.py:105
  79.3 21.4 %all-to-all-start.3 = ((bf16[32,8,1280]{2,1,0:T(8,128)(2,1)}), bf16[32,8,1280]{2,1,0:T(8,128)(2,1)S(1)}, u32[]{:S(2)}, u32[]{:S(2)}) async-start(bf16[32,8,1280]{2,1,0:T(8,128)(2,1)} %fusion.12), calls=%async_computation.3 | async-start | bytes 1310720 | tf_op jit(solution)/shard_map/all_to_all | solution.py:112
  102.2 21.5 %all-to-all-start.4 = ((bf16[32,8,1280]{2,1,0:T(8,128)(2,1)}), bf16[32,8,1280]{2,1,0:T(8,128)(2,1)}, u32[]{:S(2)}, u32[]{:S(2)}) async-start(bf16[32,8,1280]{2,1,0:T(8,128)(2,1)} %fusion.13), calls=%async_computation.4 | async-start | bytes 1310720 | tf_op jit(solution)/shard_map/all_to_all | solution.py:116
  106.1 156.9 %all-reduce.6.cloned.1.call-start = ((), (), s32[]{:S(2)}) async-start(), calls=%async_computation.5 | async-start | bytes 196608 | tf_op jit(solution)/shard_map/psum | solution.py:127
  128.9 4.4 %copy-start.3 = (bf16[512,10,2,64]{0,3,2,1:T(8,128)(2,1)S(1)}, bf16[512,10,2,64]{0,3,2,1:T(8,128)(2,1)}, u32[]{:S(2)}) copy-start(bf16[512,10,2,64]{0,3,2,1:T(8,128)(2,1)} %copy-done.2) | copy-start | bytes 3932164
  128.9 4.4 %copy-start.4 = (bf16[512,1280]{0,1:T(8,128)(2,1)S(1)}, bf16[512,1280]{0,1:T(8,128)(2,1)}, u32[]{:S(2)}) copy-start(bf16[512,1280]{0,1:T(8,128)(2,1)} %copy.46) | copy-start | bytes 3932164
  128.9 4.9 %copy-start.10 = (bf16[512,10,2,64]{0,3,2,1:T(8,128)(2,1)S(1)}, bf16[512,10,2,64]{0,3,2,1:T(8,128)(2,1)}, u32[]{:S(2)}) copy-start(bf16[512,10,2,64]{0,3,2,1:T(8,128)(2,1)} %copy-done.9) | copy-start | bytes 3932164
  133.2 1.3 copy-start.6
  133.2 1.7 copy-start.8
Sparse Core Ops, SparseCore 0:
  141.6 121.3 all-reduce.5
where the time goes:
time: 272 us; the launch traced here: 271 us
  waiting for transfers between devices  139 us (51%)
  blocking collectives  39.5 us (15%)
  matrix products  28.4 us (10%)
  starting transfers between devices  23.7 us (9%)
  local copies, waits for them, and re-layouts  18.3 us (7%)
  between operations  14.4 us (5%)
  other arithmetic  8.34 us (3%)
    psum x1, waiting for transfers between devices, body(): lax.psum((g_conv, g_bias, g_theta), ('region', 'sub'))  73.8 us
    psum x1, blocking collectives, body(): lax.psum((g_conv, g_bias, g_theta), ('region', 'sub'))  39.5 us
    all_to_all x1, waiting for transfers between devices, body(): lax.all_to_all(send_grads, ('region', 'sub'), split_axis=0, concat_axis=0...  17.2 us
    all_to_all x1, waiting for transfers between devices, body(): lax.all_to_all(ret_grads, ('region', 'sub'), split_axis=0, concat_axis=0,...  16.9 us
    all_to_all x1, waiting for transfers between devices, body(): lax.all_to_all(send, ('region', 'sub'), split_axis=0, concat_axis=0, tile...  15.4 us
    all_to_all x1, waiting for transfers between devices, body(): lax.all_to_all(ret_rows, ('region', 'sub'), split_axis=0, concat_axis=0,...  15.4 us
    unnamed x32, local copies, waits for them, and re-layouts  7.5 us
    dot_general x2, matrix products, member_side(): jnp.dot(members, back, preferred_element_type=jnp.float32)  6.71 us
  transfers between devices with their start and end apart: 6, of which 5 were waited for; matrix products, arithmetic and copies ran while one was open for 7% of the time, Pallas kernels for 0%

commit v1 on v0

--- a/solution.py
+++ b/solution.py
@@ -10,6 +10,11 @@
 MEM = 2
 TP = 10
 EDGE_DEV = 128
+
+
+def one_after_other(x, axis_one, axis_two):
+    half = lax.psum(x, axis_one)
+    return lax.psum(half, axis_two)
 
 
 def body(
@@ -124,7 +129,7 @@
     )
     g_conv = jnp.einsum("stbk,stbf->kf", stack, du, preferred_element_type=jnp.float32)
     g_bias = jnp.sum(du.astype(jnp.float32), axis=(0, 1, 2))
-    sum_conv, sum_bias, sum_theta = lax.psum((g_conv, g_bias, g_theta), ("region", "sub"))
+    sum_conv, sum_bias, sum_theta = one_after_other((g_conv, g_bias, g_theta), "sub", "region")
     norm = 1.0 / jnp.sqrt(jnp.float32(seg * device_list * TP * B))
     dstack = jnp.einsum("stbf,kf->stbk", du, conv_weight, preferred_element_type=jnp.float32)
     grad_sum = jnp.zeros((seg, T_SIZE, B, C), jnp.float32)

time: 272 us -> 240 us (0.88)
  waiting for transfers between devices: 139 us -> 98.6 us
  local copies, waits for them, and re-layouts: 18.3 us -> 22.1 us
  other arithmetic: 8.34 us -> 11.7 us
    psum x1 -> x2, waiting for transfers between devices: 73.8 us -> 33.7 us  [the longest x1 30.4 us: one_after_other(): return lax.psum(half, axis_two)]
    convert_element_type x1, other arithmetic: 1 us -> 4.4 us  [body(): grad_feats = grad_sum.astype(jnp.bfloat16).reshape(seg, T_SIZE * B * C)]
    slice x1, local copies, waits for them, and re-layouts: 4.41 us -> 7.15 us  [body(): dstack[..., k * C:(k + 1) * C]]
    psum x1 -> x2, blocking collectives: 39.5 us -> 38.9 us  [the longest x1 22.7 us: one_after_other(): half = lax.psum(x, axis_one)]
  transfers between devices with their start and end apart: 6 -> 7, of which waited for: 5 -> 6; matrix products, arithmetic and copies ran while one was open for 7% -> 12% of each run, Pallas kernels for 0% -> 0%
where the time goes in v1:
time: 240 us; the launch traced here: 238 us
  waiting for transfers between devices  98.6 us (41%)
  blocking collectives  38.9 us (16%)
  matrix products  28.4 us (12%)
  starting transfers between devices  23.7 us (10%)
  local copies, waits for them, and re-layouts  22.1 us (9%)
  between operations  14.4 us (6%)
  other arithmetic  11.7 us (5%)
    psum x1, waiting for transfers between devices, one_after_other(): return lax.psum(half, axis_two)  30.4 us
    psum x1, blocking collectives, one_after_other(): half = lax.psum(x, axis_one)  22.7 us
    all_to_all x1, waiting for transfers between devices, body(): lax.all_to_all(send_grads, ('region', 'sub'), split_axis=0, concat_axis=0...  17.2 us
    all_to_all x1, waiting for transfers between devices, body(): lax.all_to_all(ret_grads, ('region', 'sub'), split_axis=0, concat_axis=0,...  16.9 us
    psum x1, blocking collectives, one_after_other(): return lax.psum(half, axis_two)  16.2 us
    all_to_all x1, waiting for transfers between devices, body(): lax.all_to_all(send, ('region', 'sub'), split_axis=0, concat_axis=0, tile...  15.4 us
    all_to_all x1, waiting for transfers between devices, body(): lax.all_to_all(ret_rows, ('region', 'sub'), split_axis=0, concat_axis=0,...  15.4 us
    unnamed x32, local copies, waits for them, and re-layouts  8.53 us
  transfers between devices with their start and end apart: 7, of which 6 were waited for; matrix products, arithmetic and copies ran while one was open for 12% of the time, Pallas kernels for 0%

profile of v1, /device:TPU:8, one launch (start us, length us, event | category | flops | bytes accessed | tf_op | source)
XLA Modules:
  0.0 237.8 jit_solution(9706555793400806454)
XLA Ops:
  11.4 6.0 %all-to-all-start = ((s32[32,8,1]{1,2,0:T(1,128)}), s32[32,8,1]{1,2,0:T(1,128)S(1)}, u32[]{:S(2)}, u32[]{:S(2)}) async-start(s32[32,8,1]{1,2,0:T(1,128)} %bitcast.5), calls=%async_computation | async-start | bytes 32768 | tf_op jit(solution)/shard_map/all_to_all | solution.py:85
  18.6 1.7 copy.44
  27.6 5.8 %all-to-all-start.1 = ((bf16[32,8,1280]{2,1,0:T(8,128)(2,1)}), bf16[32,8,1280]{2,1,0:T(8,128)(2,1)S(1)}, u32[]{:S(2)}, u32[]{:S(2)}) async-start(bf16[32,8,1280]{2,1,0:T(8,128)(2,1)} %fusion.10), calls=%async_computation.1 | async-start | bytes 1310720 | tf_op jit(solution)/shard_map/all_to_all | solution.py:84
  35.6 15.4 %all-to-all-done.1 = bf16[32,8,1280]{2,1,0:T(8,128)(2,1)S(1)} async-done(((bf16[32,8,1280]{2,1,0:T(8,128)(2,1)}), bf16[32,8,1280]{2,1,0:T(8,128)(2,1)S(1)}, u32[]{:S(2)}, u32[]{:S(2)}) %all-to-all-start.1) | async-done | bytes 655392 | tf_op jit(solution)/shard_map/all_to_all | solution.py:84
  52.5 3.8 %all-to-all-start.2 = ((bf16[32,8,1280]{2,1,0:T(8,128)(2,1)}), bf16[32,8,1280]{2,1,0:T(8,128)(2,1)S(1)}, u32[]{:S(2)}, u32[]{:S(2)}) async-start(bf16[32,8,1280]{2,1,0:T(8,128)(2,1)} %fusion.11), calls=%async_computation.2 | async-start | bytes 1310720 | tf_op jit(solution)/shard_map/all_to_all | solution.py:110
  56.5 2.1 fusion.43
  58.5 15.4 %all-to-all-done.2 = bf16[32,8,1280]{2,1,0:T(8,128)(2,1)S(1)} async-done(((bf16[32,8,1280]{2,1,0:T(8,128)(2,1)}), bf16[32,8,1280]{2,1,0:T(8,128)(2,1)S(1)}, u32[]{:S(2)}, u32[]{:S(2)}) %all-to-all-start.2) | async-done | bytes 655392 | tf_op jit(solution)/shard_map/all_to_all | solution.py:110
  73.9 4.0 %divide_convert_fusion = (bf16[512,1280]{1,0:T(8,128)(2,1)S(1)}, bf16[512,1280]{1,0:T(8,128)(2,1)}) fusion(bf16[512,1280]{1,0:T(8,128)(2,1)} %param.19, f32[512]{0:T(512)S(1)} %broadcast_add_fusion.1, f32[512,1280]{1,0:T(8,128)} %fusion.43, bf16[32,8,1280]{2,1,0:T(8,128)(2,1)S(1)} %all-to-all-done.2, s32[256]{0:T(256)S(1)} %scatter_custom_fusion.1), kind=kOutput, calls=%fused_computation.19 | convolution fusion | flops 345767936 | bytes 7212032 | tf_op jit(solution)/shard_map/dot_general | solution.py:107
  79.3 3.8 %all-to-all-start.3 = ((bf16[32,8,1280]{2,1,0:T(8,128)(2,1)}), bf16[32,8,1280]{2,1,0:T(8,128)(2,1)S(1)}, u32[]{:S(2)}, u32[]{:S(2)}) async-start(bf16[32,8,1280]{2,1,0:T(8,128)(2,1)} %fusion.12), calls=%async_computation.3 | async-start | bytes 1310720 | tf_op jit(solution)/shard_map/all_to_all | solution.py:117
  83.5 17.2 %all-to-all-done.3 = bf16[32,8,1280]{2,1,0:T(8,128)(2,1)S(1)} async-done(((bf16[32,8,1280]{2,1,0:T(8,128)(2,1)}), bf16[32,8,1280]{2,1,0:T(8,128)(2,1)S(1)}, u32[]{:S(2)}, u32[]{:S(2)}) %all-to-all-start.3) | async-done | bytes 655392 | tf_op jit(solution)/shard_map/all_to_all | solution.py:117
  102.2 3.9 %all-to-all-start.4 = ((bf16[32,8,1280]{2,1,0:T(8,128)(2,1)}), bf16[32,8,1280]{2,1,0:T(8,128)(2,1)}, u32[]{:S(2)}, u32[]{:S(2)}) async-start(bf16[32,8,1280]{2,1,0:T(8,128)(2,1)} %fusion.13), calls=%async_computation.4 | async-start | bytes 1310720 | tf_op jit(solution)/shard_map/all_to_all | solution.py:121
  106.9 16.9 %all-to-all-done.4 = bf16[32,8,1280]{2,1,0:T(8,128)(2,1)} async-done(((bf16[32,8,1280]{2,1,0:T(8,128)(2,1)}), bf16[32,8,1280]{2,1,0:T(8,128)(2,1)}, u32[]{:S(2)}, u32[]{:S(2)}) %all-to-all-start.4) | async-done | bytes 655392 | tf_op jit(solution)/shard_map/all_to_all | solution.py:121
  123.8 2.7 %fusion.3 = bf16[512,1280]{1,0:T(8,128)(2,1)} fusion(f32[512,1280]{1,0:T(8,128)S(1)} %fusion.39, bf16[32,8,1280]{2,1,0:T(8,128)(2,1)} %all-to-all-done.4, s32[256]{0:T(256)S(1)} %scatter_custom_fusion.1), kind=kOutput, calls=%fused_computation.10 | convolution fusion | flops 337248256 | bytes 4588544 | tf_op jit(solution)/shard_map/dot_general | solution.py:107
  126.4 2.4 %copy.46 = bf16[512,1280]{0,1:T(8,128)(2,1)} copy(bf16[512,1280]{1,0:T(8,128)(2,1)} %fusion.3) | data formatting | bytes 2621440 | tf_op jit(solution)/shard_map/convert_element_type | solution.py:124
  128.9 4.4 %multiply_convert_fusion.1 = (bf16[512,10,2,64]{0,3,2,1:T(8,128)(2,1)S(1)}, bf16[512,10,2,64]{0,3,2,1:T(8,128)(2,1)S(1)}) fusion(f32[512,10,2,128]{0,3,2,1:T(8,128)} %copy-done.1, bf16[512,10,2,64]{0,3,2,1:T(8,128)(2,1)} %bitcast.78, bf16[64,64]{1,0:T(8,128)(2,1)S(1)} %copy-done.11), kind=kOutput, calls=%fused_computation.18 | convolution fusion | flops 90439680 | bytes 9183232 | tf_op jit(solution)/shard_map/stbd,cd->stbc/dot_general | solution.py:126
  135.0 1.8 fusion.19
  137.2 4.3 %fusion.60 = f32[512,10,2,192]{0,3,2,1:T(8,128)} fusion(bf16[192,128]{1,0:T(8,128)(2,1)S(1)} %copy-done, bf16[512,10,2,64]{0,3,2,1:T(8,128)(2,1)S(1)} %get-tuple-element.33, bf16[512,10,2,64]{0,3,2,1:T(8,128)(2,1)S(1)} %get-tuple-element.32), kind=kOutput, calls=%fused_computation.82 | convolution fusion | flops 508559360 | bytes 10534912 | tf_op jit(solution)/shard_map/stbf,kf->stbk/dot_general | solution.py:134
  141.6 22.7 %all-reduce.3 = (f32[128]{0:T(128)S(1)}, f32[64,64]{1,0:T(8,128)S(1)}) all-reduce(f32[128]{0:T(128)S(1)} %convert_reduce_fusion, f32[64,64]{1,0:T(8,128)S(1)} %fusion.24), channel_id=1, replica_groups=mesh['region'=4,'sub'=8] {'sub'}, use_global_device_ids=true, to_apply=%region_10.11 | all-reduce | flops 4224 | bytes 33792 | tf_op jit(solution)/shard_map/psum | solution.py:16
  164.3 16.2 %all-reduce.4 = (f32[128]{0:T(128)S(1)}, f32[64,64]{1,0:T(8,128)S(1)}) all-reduce(f32[128]{0:T(128)S(1)} %get-tuple-element.25, f32[64,64]{1,0:T(8,128)S(1)} %get-tuple-element.26), channel_id=1, replica_groups=mesh['region'=4,'sub'=8] {'region'}, use_global_device_ids=true, to_apply=%region_11.12 | all-reduce | flops 4224 | bytes 33792 | tf_op jit(solution)/shard_map/psum | solution.py:17
  181.1 7.1 %fusion.71 = (f32[512,10,2,64]{0,3,2,1:T(8,128)S(1)}, f32[512,10,2,64]{0,3,2,1:T(8,128)}, f32[512,10,2,64]{0,3,2,1:T(8,128)}) fusion(f32[512,10,2,192]{0,3,2,1:T(8,128)} %fusion.60), kind=kLoop, calls=%fused_computation.100 | loop fusion | bytes 15728640 | tf_op jit(solution)/shard_map/slice | solution.py:138
  188.8 3.3 %all-reduce.8.cloned.1.call-done = f32[192,128]{1,0:T(8,128)} async-done(((f32[192,128]{1,0:T(8,128)}), f32[192,128]{1,0:T(8,128)}) %all-reduce.8.cloned.1.call-update) | async-done | bytes 98320 | tf_op jit(solution)/shard_map/psum | solution.py:16
  192.1 4.4 %add_convert_fusion = bf16[512,12,2,64]{0,3,2,1:T(8,128)(2,1)} fusion(f32[512,10,2,64]{0,3,2,1:T(8,128)} %get-tuple-element.30, f32[512,10,2,64]{0,3,2,1:T(8,128)} %get-tuple-element.31, f32[512,10,2,64]{0,3,2,1:T(8,128)S(1)} %get-tuple-element.29), kind=kLoop, calls=%fused_computation.9 | loop fusion | flops 2359296 | bytes 9437184 | tf_op jit(solution)/shard_map/convert_element_type | solution.py:140
  196.5 2.6 %copy.52 = bf16[512,1536]{1,0:T(8,128)(2,1)} copy(bf16[512,1536]{0,1:T(8,128)(2,1)} %bitcast.77) | data formatting | bytes 3145728
  199.1 30.4 %all-reduce.10.cloned.1.call-done = f32[192,128]{1,0:T(8,128)} async-done(((f32[192,128]{1,0:T(8,128)}), f32[192,128]{1,0:T(8,128)}) %all-reduce.10.cloned.1.call-update) | async-done | bytes 98320 | tf_op jit(solution)/shard_map/psum | solution.py:17
  (69 shorter events, 25.0 us)
Async XLA Ops:
  7.2 13.7 %copy-start = (bf16[192,128]{1,0:T(8,128)(2,1)S(1)}, bf16[192,128]{1,0:T(8,128)(2,1)}, u32[]{:S(2)}) copy-start(bf16[192,128]{1,0:T(8,128)(2,1)} %param.11) | copy-start | bytes 147460
  11.4 16.1 %all-to-all-start = ((s32[32,8,1]{1,2,0:T(1,128)}), s32[32,8,1]{1,2,0:T(1,128)S(1)}, u32[]{:S(2)}, u32[]{:S(2)}) async-start(s32[32,8,1]{1,2,0:T(1,128)} %bitcast.5), calls=%async_computation | async-start | bytes 32768 | tf_op jit(solution)/shard_map/all_to_all | solution.py:85
  20.3 0.7 copy-start.14
  20.8 1.2 copy-start.5
  20.8 1.6 copy-start.7
  20.8 1.9 copy-start.9
  22.7 2.3 copy-start.1
  22.7 2.3 copy-start.11
  25.0 1.1 copy-start.2
  25.1 8.4 %copy-start.12 = (s32[512,2]{0,1:T(2,128)S(1)}, s32[512,2]{0,1:T(2,128)}, u32[]{:S(2)}) copy-start(s32[512,2]{0,1:T(2,128)} %param.15) | copy-start | bytes 12292
  26.2 9.4 %copy-start.13 = (f32[128]{0:T(128)S(1)}, f32[128]{0:T(128)}, u32[]{:S(2)}) copy-start(f32[128]{0:T(128)} %param.14) | copy-start | bytes 1540
  27.6 23.4 %all-to-all-start.1 = ((bf16[32,8,1280]{2,1,0:T(8,128)(2,1)}), bf16[32,8,1280]{2,1,0:T(8,128)(2,1)S(1)}, u32[]{:S(2)}, u32[]{:S(2)}) async-start(bf16[32,8,1280]{2,1,0:T(8,128)(2,1)} %fusion.10), calls=%async_computation.1 | async-start | bytes 1310720 | tf_op jit(solution)/shard_map/all_to_all | solution.py:84
  52.5 21.4 %all-to-all-start.2 = ((bf16[32,8,1280]{2,1,0:T(8,128)(2,1)}), bf16[32,8,1280]{2,1,0:T(8,128)(2,1)S(1)}, u32[]{:S(2)}, u32[]{:S(2)}) async-start(bf16[32,8,1280]{2,1,0:T(8,128)(2,1)} %fusion.11), calls=%async_computation.2 | async-start | bytes 1310720 | tf_op jit(solution)/shard_map/all_to_all | solution.py:110
  79.3 21.4 %all-to-all-start.3 = ((bf16[32,8,1280]{2,1,0:T(8,128)(2,1)}), bf16[32,8,1280]{2,1,0:T(8,128)(2,1)S(1)}, u32[]{:S(2)}, u32[]{:S(2)}) async-start(bf16[32,8,1280]{2,1,0:T(8,128)(2,1)} %fusion.12), calls=%async_computation.3 | async-start | bytes 1310720 | tf_op jit(solution)/shard_map/all_to_all | solution.py:117
  102.2 21.5 %all-to-all-start.4 = ((bf16[32,8,1280]{2,1,0:T(8,128)(2,1)}), bf16[32,8,1280]{2,1,0:T(8,128)(2,1)}, u32[]{:S(2)}, u32[]{:S(2)}) async-start(bf16[32,8,1280]{2,1,0:T(8,128)(2,1)} %fusion.13), calls=%async_computation.4 | async-start | bytes 1310720 | tf_op jit(solution)/shard_map/all_to_all | solution.py:121
  106.1 85.9 %all-reduce.8.cloned.1.call-start = ((), (), s32[]{:S(2)}) async-start(), calls=%async_computation.5 | async-start | bytes 196608 | tf_op jit(solution)/shard_map/psum | solution.py:16
  128.9 4.4 %copy-start.3 = (bf16[512,10,2,64]{0,3,2,1:T(8,128)(2,1)S(1)}, bf16[512,10,2,64]{0,3,2,1:T(8,128)(2,1)}, u32[]{:S(2)}) copy-start(bf16[512,10,2,64]{0,3,2,1:T(8,128)(2,1)} %copy-done.2) | copy-start | bytes 3932164
  128.9 4.4 %copy-start.4 = (bf16[512,1280]{0,1:T(8,128)(2,1)S(1)}, bf16[512,1280]{0,1:T(8,128)(2,1)}, u32[]{:S(2)}) copy-start(bf16[512,1280]{0,1:T(8,128)(2,1)} %copy.46) | copy-start | bytes 3932164
  128.9 4.9 %copy-start.10 = (bf16[512,10,2,64]{0,3,2,1:T(8,128)(2,1)S(1)}, bf16[512,10,2,64]{0,3,2,1:T(8,128)(2,1)}, u32[]{:S(2)}) copy-start(bf16[512,10,2,64]{0,3,2,1:T(8,128)(2,1)} %copy-done.9) | copy-start | bytes 3932164
  133.3 1.3 copy-start.6
  133.3 1.7 copy-start.8
  141.5 88.0 %all-reduce.10.cloned.1.call-start = ((), (), s32[]{:S(2)}) async-start(), calls=%async_computation.6 | async-start | bytes 196608 | tf_op jit(solution)/shard_map/psum | solution.py:17
Sparse Core Ops, SparseCore 0:
  141.6 50.3 all-reduce.7
  194.5 34.9 all-reduce.9
